TPU v7x, 128 devices: a whole 4x4x4 slice. The times are simulated.
128 devices in a mesh: blk: 16 (over y_hi, x, core), reg: 8 (over z, y_lo).
Axes of the slice: x: 4, y: 4 (y_hi: 2, y_lo: 2; y = y_hi * 2 + y_lo), z: 4, core: 2. Of those that a mesh axis runs over, the one named last changes fastest.
Arguments:
- inv_factor: bfloat16 [256, 1024, 1024], P(('blk', 'reg')), may hold values from -0.1875 to 0.1875
- border_global: bfloat16 [256, 1024, 512], P(('blk', 'reg')), may hold values from -6 to 6
- border_local: bfloat16 [256, 1024, 1536], P(('blk', 'reg')), may hold values from -6 to 6
- local_count: int32 [256], P(('blk', 'reg')), may hold values from 512 to 1536, as said below
Outputs:
- schur_global: float32 [512, 512], P('blk')
- schur_local: float32 [8, 1536, 1536], P('reg', 'blk')
- schur_cross: float32 [8, 512, 1536], P('reg', 'blk')
Inputs may be any that keep to these rules, and one draw needn't show every extreme that they name: Each block touches the first local_count of its region's local linking columns; some block touches exactly 1536 and some exactly 512.
All inputs are finite; a program needn't handle non-finite values.
Results may differ from a plain program's by a relative error of at most 0.0039.
Values may be sent and summed in bfloat16 or wider, within the bound.
No kernel may reach another device: no remote copies, remote signals or barrier semaphores. Data moves between devices by JAX's collectives and lax.ppermute only.
A program may use at most 128 MiB of HBM per device.

v0:
```python
import math

import jax
import jax.numpy as jnp
import numpy as np
from jax import lax
from jax.sharding import Mesh
from jax.sharding import PartitionSpec as P


BLK_AXES = ("yh", "x", "core")
REG_AXES = ("z", "yl")
CHIP_AXES = ("yh", "x")


def left_products(factor, border):
    return lax.dot_general(
        border, factor, (((1,), (1,)), ((0,), (0,))), preferred_element_type=jnp.float32
    ).astype(jnp.bfloat16)


def gram(first, second):
    return lax.dot_general(
        first, second, (((0, first.ndim - 1), (0, second.ndim - 1)), ((), ())),
        preferred_element_type=jnp.float32,
    )


def chip_exchange(send):
    n_yh = lax.axis_size("yh")
    n_x = lax.axis_size("x")
    yh = lax.axis_index("yh")
    x = lax.axis_index("x")
    total = lax.dynamic_index_in_dim(send, yh * n_x + x, 0, False).astype(jnp.float32)
    for flip in range(n_yh):
        for shift in range(n_x):
            if flip == 0 and shift == 0:
                continue
            dest = (yh ^ flip) * n_x + (x + shift) % n_x
            pairs = [
                (a * n_x + b, (a ^ flip) * n_x + (b + shift) % n_x) for a in range(n_yh) for b in range(n_x)
            ]
            piece = lax.dynamic_index_in_dim(send, dest, 0, False)
            total = total + lax.ppermute(piece, CHIP_AXES, pairs).astype(jnp.float32)
    return total


def shards_body(inv_factor, border_global, border_local, local_count):
    blk_dev, order, _ = inv_factor.shape
    global_cols = border_global.shape[2]
    local_cols = border_local.shape[2]
    n_core = lax.axis_size("core")
    n_chip = lax.axis_size("yh") * lax.axis_size("x")
    n_blk = n_core * n_chip
    n_reg = lax.axis_size("z") * lax.axis_size("yl")

    columns = jnp.arange(local_cols, dtype=jnp.int32)
    masked = jnp.where(
        columns[None, None, :] < local_count[:, None, None], border_local, jnp.zeros((), border_local.dtype)
    )
    left_g = left_products(inv_factor, border_global)
    left_l = left_products(inv_factor, masked)

    rows_g = global_cols // n_blk
    rows_l = local_cols // n_blk
    core = lax.axis_index("core")
    by_owner_g = left_g.reshape(blk_dev, n_chip, n_core, rows_g, order)
    by_owner_l = left_l.reshape(blk_dev, n_chip, n_core, rows_l, order)

    def pick(by_owner, which):
        return lax.dynamic_index_in_dim(by_owner, which, 2, keepdims=False)

    swap = [(0, 1), (1, 0)]
    sib_g = pick(by_owner_g, 1 - core)
    sib_gg = lax.ppermute(gram(sib_g, left_g), "core", swap)
    sib_gl = lax.ppermute(gram(sib_g, left_l), "core", swap)
    own_g = pick(by_owner_g, core)
    own_gg, own_gl = lax.optimization_barrier((gram(own_g, left_g), gram(own_g, left_l)))
    send_top = jnp.concatenate([own_gg + sib_gg, own_gl + sib_gl], axis=2).astype(jnp.bfloat16)
    send_top, late_l = lax.optimization_barrier((send_top, left_l))
    summed_top = chip_exchange(send_top)
    sib_ll_part = gram(pick(by_owner_l, 1 - core), late_l)
    sib_ll = lax.ppermute(sib_ll_part, "core", swap)
    own_ll = lax.optimization_barrier(gram(pick(by_owner_l, core), late_l))
    send_ll = (own_ll + sib_ll).astype(jnp.bfloat16)
    top_rows = summed_top[:, :global_cols]
    send_ll, top_rows = lax.optimization_barrier((send_ll, top_rows))
    low = chip_exchange(send_ll)
    top = top_rows
    cross = summed_top[:, global_cols:]
    top = region_sum(top)
    all_blocks = blk_dev * n_blk * n_reg
    global_scale = 1.0 / math.sqrt(order * all_blocks)
    region_scale = 1.0 / math.sqrt(order * blk_dev * n_blk)
    return (
        top * global_scale,
        (low * region_scale)[None],
        (cross * region_scale)[None],
    )


def region_sum(top):
    for axis in REG_AXES:
        size = lax.axis_size(axis)
        step = 1
        while step < size:
            pairs = [(i, i ^ step) for i in range(size)]
            top = top + lax.ppermute(top, axis, pairs)
            step *= 2
    return top


def solution(mesh):
    n_blk, n_reg = mesh.devices.shape
    devices = np.asarray(mesh.devices).reshape(2, n_blk // 4, 2, n_reg // 2, 2)
    fine = Mesh(devices, BLK_AXES + REG_AXES)
    every = BLK_AXES + REG_AXES
    placed = (P(every, None, None), P(every, None, None), P(every, None, None), P(every))
    return jax.shard_map(
        shards_body,
        mesh=fine,
        in_specs=placed,
        out_specs=(P(BLK_AXES, None), P(REG_AXES, BLK_AXES, None), P(REG_AXES, BLK_AXES, None)),
        check_vma=False,
    )
```

profile of v0, /device:TPU:70, one launch (start us, length us, event | category | flops | bytes accessed | tf_op | source)
XLA Modules:
  0.0 103.0 jit_solution(8286898141217157361)
XLA Ops:
  0.6 0.0 copy-start
  0.7 1.6 %copy-done = bf16[2,1024,512]{2,1,0:T(8,128)(2,1)S(1)} copy-done((bf16[2,1024,512]{2,1,0:T(8,128)(2,1)S(1)}, bf16[2,1024,512]{2,1,0:T(8,128)(2,1)}, u32[]{:S(2)}) %copy-start) | copy-done | bytes 2097176
  2.2 4.5 %convolution_convert_fusion = bf16[2,512,1024]{2,1,0:T(8,128)(2,1)S(1)} fusion(bf16[2,1024,512]{2,1,0:T(8,128)(2,1)S(1)} %copy-done, bf16[2,1024,1024]{2,1,0:T(8,128)(2,1)} %param.4), kind=kOutput, calls=%fused_computation.26 | convolution fusion | flops 2148532224 | bytes 8388608 | tf_op jit(solution)/shard_map/dot_general | solution.py:17
  6.8 0.0 slice-start
  6.8 0.3 constant_dynamic-slice_fusion.1
  7.1 0.0 copy-start.2
  7.1 0.0 slice-start.1
  7.1 0.0 copy-start.3
  7.1 0.7 fusion.38
  7.9 0.1 collective-permute-start
  8.0 0.1 iota_compare_fusion
  8.0 0.9 slice-done
  9.0 0.8 slice-done.1
  9.7 1.2 %copy-done.3 = bf16[2,1024,1024]{2,1,0:T(8,128)(2,1)S(1)} copy-done((bf16[2,1024,1024]{2,1,0:T(8,128)(2,1)S(1)}, bf16[2,1024,1024]{2,1,0:T(8,128)(2,1)}, u32[]{:S(2)}) %copy-start.3) | copy-done | bytes 4194328
  10.9 7.2 %fusion.11 = bf16[2,1536,1024]{2,1,0:T(8,128)(2,1)S(1)} fusion(bf16[2,1024,1024]{2,1,0:T(8,128)(2,1)S(1)} %copy-done.3, bf16[2,1024,1536]{2,1,0:T(8,128)(2,1)S(1)} %bitcast.107, pred[2,1536]{1,0:T(4,128)(4,1)S(1)} %iota_compare_fusion), kind=kOutput, calls=%fused_computation.11 | convolution fusion | flops 6448742400 | bytes 16780288 | tf_op jit(solution)/shard_map/dot_general | solution.py:17
  18.2 1.8 %fusion.28 = f32[8,32,1536]{2,1,0:T(8,128)S(1)} fusion(bf16[2,1536,1024]{2,1,0:T(8,128)(2,1)S(1)} %fusion.11, bf16[2,8,1,32,1024]{4,3,2,1,0:T(8,128)(2,1)S(1)} %get-tuple-element.24), kind=kOutput, calls=%fused_computation.21 | convolution fusion | flops 1610612736 | bytes 8912896 | tf_op jit(solution)/shard_map/dot_general | solution.py:23
  20.0 0.3 collective-permute-start.1
  20.3 1.8 %fusion.25 = f32[8,32,1536]{2,1,0:T(8,128)S(1)} fusion(bf16[2,1536,1024]{2,1,0:T(8,128)(2,1)S(1)} %fusion.11, bf16[2,8,1,32,1024]{4,3,2,1,0:T(8,128)(2,1)S(1)} %get-tuple-element.25), kind=kOutput, calls=%fused_computation.20 | convolution fusion | flops 1610612736 | bytes 8912896 | tf_op jit(solution)/shard_map/dot_general | solution.py:23
  22.1 0.7 fusion.35
  22.9 2.7 %constant_dynamic-slice_fusion = (bf16[2,8,1,96,1024]{4,3,2,1,0:T(8,128)(2,1)S(1)}, bf16[2,8,1,96,1024]{4,3,2,1,0:T(8,128)(2,1)}) fusion(bf16[2,8,2,96,1024]{4,3,2,1,0:T(8,128)(2,1)S(1)} %bitcast.104, s32[]{:T(128)S(6)} %select_n.89, s32[]{:T(128)S(6)} %select_n.88), kind=kLoop, calls=%fused_computation.74 | loop fusion | bytes 12582920 | tf_op jit(solution)/shard_map/jit(dynamic_index_in_dim)/dynamic_slice | solution.py:71
  25.6 0.0 collective-permute-done
  25.6 0.1 add_convert_fusion.2
  25.7 0.0 collective-permute-done.1
  25.7 0.2 add_convert_fusion.1
  25.9 0.1 pad_maximum_fusion
  26.1 6.8 %fusion.17 = f32[8,96,1536]{2,1,0:T(8,128)} fusion(bf16[2,1536,1024]{2,1,0:T(8,128)(2,1)S(1)} %fusion.11, bf16[2,8,1,96,1024]{4,3,2,1,0:T(8,128)(2,1)S(1)} %get-tuple-element.15), kind=kOutput, calls=%fused_computation.14 | convolution fusion | flops 4831838208 | bytes 14155776 | tf_op jit(solution)/shard_map/dot_general | solution.py:23
  32.9 0.5 collective-permute-start.2
  33.4 0.9 dynamic-slice_bitcast_fusion.13
  34.3 0.5 collective-permute-start.3
  34.8 4.2 %collective-permute-start.9 = (bf16[32,2048]{1,0:T(8,128)(2,1)}, bf16[32,2048]{1,0:T(8,128)(2,1)S(1)}, u32[]{:S(2)}, u32[]{:S(2)}) collective-permute-start(bf16[32,2048]{1,0:T(8,128)(2,1)} %get-tuple-element.27), channel_id=1, source_target_pairs={{0,112},{16,64},{32,80},{48,96},{64,48},{80,0},{96,16},{112,32},{1... | collective-permute-start | bytes 393224 | tf_op jit(solution)/shard_map/ppermute | solution.py:44
  39.0 1.2 %collective-permute-start.8 = (bf16[32,2048]{1,0:T(8,128)(2,1)}, bf16[32,2048]{1,0:T(8,128)(2,1)}, u32[]{:S(2)}, u32[]{:S(2)}) collective-permute-start(bf16[32,2048]{1,0:T(8,128)(2,1)} %get-tuple-element.28), channel_id=1, source_target_pairs={{0,96},{16,112},{32,64},{48,80},{64,32},{80,48},{96,0},{112,16},{1... | collective-permute-start | bytes 393224 | tf_op jit(solution)/shard_map/ppermute | solution.py:44
  40.1 4.7 %collective-permute-start.7 = (bf16[32,2048]{1,0:T(8,128)(2,1)}, bf16[32,2048]{1,0:T(8,128)(2,1)S(1)}, u32[]{:S(2)}, u32[]{:S(2)}) collective-permute-start(bf16[32,2048]{1,0:T(8,128)(2,1)} %get-tuple-element.29), channel_id=1, source_target_pairs={{0,80},{16,96},{32,112},{48,64},{64,16},{80,32},{96,48},{112,0},{1... | collective-permute-start | bytes 393224 | tf_op jit(solution)/shard_map/ppermute | solution.py:44
  44.9 0.3 collective-permute-start.6
  45.2 0.0 collective-permute-start.5
  45.2 4.3 %collective-permute-done.8 = bf16[32,2048]{1,0:T(8,128)(2,1)} collective-permute-done((bf16[32,2048]{1,0:T(8,128)(2,1)}, bf16[32,2048]{1,0:T(8,128)(2,1)}, u32[]{:S(2)}, u32[]{:S(2)}) %collective-permute-start.8) | collective-permute-done | bytes 131104 | tf_op jit(solution)/shard_map/ppermute | solution.py:44
  49.5 0.9 collective-permute-start.4
  50.4 8.2 %fusion.14 = f32[8,96,1536]{2,1,0:T(8,128)S(1)} fusion(bf16[2,1536,1024]{2,1,0:T(8,128)(2,1)} %copy-done.1, bf16[2,8,1,96,1024]{4,3,2,1,0:T(8,128)(2,1)} %get-tuple-element.16), kind=kOutput, calls=%fused_computation.13 | convolution fusion | flops 4831838208 | bytes 14155776 | tf_op jit(solution)/shard_map/dot_general | solution.py:23
  58.6 0.0 collective-permute-done.6
  58.6 0.0 collective-permute-done.5
  58.6 1.0 %fusion.62 = f32[32,2048]{1,0:T(8,128)S(1)} fusion(bf16[32,2048]{1,0:T(8,128)(2,1)S(1)} %collective-permute-done.9, bf16[32,2048]{1,0:T(8,128)(2,1)} %collective-permute-done.8, bf16[32,2048]{1,0:T(8,128)(2,1)S(1)} %collective-permute-done.7, bf16[32,2048]{1,0:T(8,128)(2,1)S(1)} %collective-permute-done.6, bf16[32,2048]{1,0:T(8,128)(2,1)S(1)} %collective-permute-done.5, ...), kind=kLoop, calls=%fused_computation.62 | loop fusion | flops 983040 | bytes 1310724 | tf_op jit(solution)/shard_map/add | solution.py:44
  59.7 0.0 collective-permute-done.2
  59.7 3.2 %add_convert_fusion = bf16[8,96,1536]{2,1,0:T(8,128)(2,1)S(1)} fusion(f32[8,96,1536]{2,1,0:T(8,128)S(1)} %fusion.14, f32[8,96,1536]{2,1,0:T(8,128)} %collective-permute-done.2), kind=kLoop, calls=%fused_computation.12 | loop fusion | flops 2359296 | bytes 11796480 | tf_op jit(solution)/shard_map/convert_element_type | solution.py:85
  62.9 0.2 dynamic-slice_bitcast_fusion.6
  63.1 2.7 %collective-permute-start.13 = (bf16[96,1536]{1,0:T(8,128)(2,1)S(1)}, bf16[96,1536]{1,0:T(8,128)(2,1)S(1)}, u32[]{:S(2)}, u32[]{:S(2)}) collective-permute-start(bf16[96,1536]{1,0:T(8,128)(2,1)S(1)} %get-tuple-element.17), channel_id=1, source_target_pairs={{0,16},{16,32},{32,48},{48,0},{64,80},{80,96},{96,112},{112,64},{1... | collective-permute-start | bytes 884744 | tf_op jit(solution)/shard_map/ppermute | solution.py:44
  65.8 2.0 %collective-permute-start.19 = (bf16[96,1536]{1,0:T(8,128)(2,1)S(1)}, bf16[96,1536]{1,0:T(8,128)(2,1)S(1)}, u32[]{:S(2)}, u32[]{:S(2)}) collective-permute-start(bf16[96,1536]{1,0:T(8,128)(2,1)S(1)} %get-tuple-element.18), channel_id=1, source_target_pairs={{0,112},{16,64},{32,80},{48,96},{64,48},{80,0},{96,16},{112,32},{1... | collective-permute-start | bytes 884744 | tf_op jit(solution)/shard_map/ppermute | solution.py:44
  67.8 1.6 %collective-permute-start.10 = (f32[32,512]{1,0:T(8,128)S(1)}, f32[32,512]{1,0:T(8,128)S(1)}, u32[]{:S(2)}, u32[]{:S(2)}) collective-permute-start(f32[32,512]{1,0:T(8,128)S(1)} %slice.8), channel_id=1, source_target_pairs={{0,2},{2,0},{4,6},{6,4},{1,3},{3,1},{5,7},{7,5},{8,10},{10,8},{12,... | collective-permute-start | bytes 196616 | tf_op jit(solution)/shard_map/ppermute | solution.py:108
  69.5 2.6 %collective-permute-done.10 = f32[32,512]{1,0:T(8,128)S(1)} collective-permute-done((f32[32,512]{1,0:T(8,128)S(1)}, f32[32,512]{1,0:T(8,128)S(1)}, u32[]{:S(2)}, u32[]{:S(2)}) %collective-permute-start.10) | collective-permute-done | bytes 65568 | tf_op jit(solution)/shard_map/ppermute | solution.py:108
  72.1 0.1 collective-permute-start.11
  72.2 5.8 %collective-permute-done.11 = f32[32,512]{1,0:T(8,128)S(1)} collective-permute-done((f32[32,512]{1,0:T(8,128)S(1)}, f32[32,512]{1,0:T(8,128)S(1)}, u32[]{:S(2)}, u32[]{:S(2)}) %collective-permute-start.11) | collective-permute-done | bytes 65568 | tf_op jit(solution)/shard_map/ppermute | solution.py:108
  78.0 0.6 collective-permute-start.12
  78.6 3.1 %collective-permute-start.18 = (bf16[96,1536]{1,0:T(8,128)(2,1)S(1)}, bf16[96,1536]{1,0:T(8,128)(2,1)S(1)}, u32[]{:S(2)}, u32[]{:S(2)}) collective-permute-start(bf16[96,1536]{1,0:T(8,128)(2,1)S(1)} %get-tuple-element.19), channel_id=1, source_target_pairs={{0,96},{16,112},{32,64},{48,80},{64,32},{80,48},{96,0},{112,16},{1... | collective-permute-start | bytes 884744 | tf_op jit(solution)/shard_map/ppermute | solution.py:44
  81.7 3.7 %collective-permute-start.17 = (bf16[96,1536]{1,0:T(8,128)(2,1)S(1)}, bf16[96,1536]{1,0:T(8,128)(2,1)S(1)}, u32[]{:S(2)}, u32[]{:S(2)}) collective-permute-start(bf16[96,1536]{1,0:T(8,128)(2,1)S(1)} %get-tuple-element.20), channel_id=1, source_target_pairs={{0,80},{16,96},{32,112},{48,64},{64,16},{80,32},{96,48},{112,0},{1... | collective-permute-start | bytes 884744 | tf_op jit(solution)/shard_map/ppermute | solution.py:44
  85.4 2.8 %collective-permute-done.12 = f32[32,512]{1,0:T(8,128)S(1)} collective-permute-done((f32[32,512]{1,0:T(8,128)S(1)}, f32[32,512]{1,0:T(8,128)S(1)}, u32[]{:S(2)}, u32[]{:S(2)}) %collective-permute-start.12) | collective-permute-done | bytes 65568 | tf_op jit(solution)/shard_map/ppermute | solution.py:108
  88.2 1.0 collective-permute-start.16
  89.2 0.0 collective-permute-done.13
  89.3 0.0 collective-permute-start.15
  89.3 0.0 collective-permute-done.19
  89.3 4.7 %collective-permute-start.14 = (bf16[96,1536]{1,0:T(8,128)(2,1)S(1)}, bf16[96,1536]{1,0:T(8,128)(2,1)S(1)}, u32[]{:S(2)}, u32[]{:S(2)}) collective-permute-start(bf16[96,1536]{1,0:T(8,128)(2,1)S(1)} %get-tuple-element.23), channel_id=1, source_target_pairs={{0,32},{16,48},{32,0},{48,16},{64,96},{80,112},{96,64},{112,80},{1... | collective-permute-start | bytes 884744 | tf_op jit(solution)/shard_map/ppermute | solution.py:44
  94.0 0.7 fusion.63
  94.7 0.6 add_multiply_fusion
  95.3 0.0 collective-permute-done.18
  95.3 3.7 %collective-permute-done.16 = bf16[96,1536]{1,0:T(8,128)(2,1)S(1)} collective-permute-done((bf16[96,1536]{1,0:T(8,128)(2,1)S(1)}, bf16[96,1536]{1,0:T(8,128)(2,1)S(1)}, u32[]{:S(2)}, u32[]{:S(2)}) %collective-permute-start.16) | collective-permute-done | bytes 294944 | tf_op jit(solution)/shard_map/ppermute | solution.py:44
  99.0 2.8 %collective-permute-done.14 = bf16[96,1536]{1,0:T(8,128)(2,1)S(1)} collective-permute-done((bf16[96,1536]{1,0:T(8,128)(2,1)S(1)}, bf16[96,1536]{1,0:T(8,128)(2,1)S(1)}, u32[]{:S(2)}, u32[]{:S(2)}) %collective-permute-start.14) | collective-permute-done | bytes 294944 | tf_op jit(solution)/shard_map/ppermute | solution.py:44
  101.8 1.1 %fusion.56 = f32[1,96,1536]{2,1,0:T(8,128)} fusion(bf16[96,1536]{1,0:T(8,128)(2,1)S(1)} %collective-permute-done.19, bf16[96,1536]{1,0:T(8,128)(2,1)S(1)} %collective-permute-done.18, bf16[96,1536]{1,0:T(8,128)(2,1)S(1)} %collective-permute-done.17, bf16[96,1536]{1,0:T(8,128)(2,1)S(1)} %collective-permute-done.16, ...), kind=kLoop, calls=%fused_computation.47 | loop fusion | flops 2359296 | bytes 2949124 | tf_op jit(solution)/shard_map/broadcast_in_dim | solution.py:97
  (13 shorter events, 0.0 us)
Async XLA Ops:
  0.6 1.6 %copy-start = (bf16[2,1024,512]{2,1,0:T(8,128)(2,1)S(1)}, bf16[2,1024,512]{2,1,0:T(8,128)(2,1)}, u32[]{:S(2)}) copy-start(bf16[2,1024,512]{2,1,0:T(8,128)(2,1)} %param.5) | copy-start | bytes 6291460
  6.8 2.2 %slice-start = ((s8[6291456]{0:T(1024)(128)(4,1)}), s8[4194304]{0:T(1024)(128)(4,1)S(1)}, s32[]{:S(2)}) async-start(s8[6291456]{0:T(1024)(128)(4,1)} %bitcast.106), calls=%async_computation | async-start | bytes 8388608
  7.1 0.9 copy-start.2
  7.1 2.7 %slice-start.1 = ((s8[6291456]{0:T(1024)(128)(4,1)}), s8[2097152]{0:T(1024)(128)(4,1)S(1)}, s32[]{:S(2)}) async-start(s8[6291456]{0:T(1024)(128)(4,1)} %bitcast.106), calls=%async_computation.1 | async-start | bytes 4194304
  7.1 3.8 %copy-start.3 = (bf16[2,1024,1024]{2,1,0:T(8,128)(2,1)S(1)}, bf16[2,1024,1024]{2,1,0:T(8,128)(2,1)}, u32[]{:S(2)}) copy-start(bf16[2,1024,1024]{2,1,0:T(8,128)(2,1)} %param.4) | copy-start | bytes 12582916
  7.9 17.7 %collective-permute-start = (f32[8,32,512]{2,1,0:T(8,128)S(1)}, f32[8,32,512]{2,1,0:T(8,128)S(1)}, u32[]{:S(2)}, u32[]{:S(2)}) collective-permute-start(f32[8,32,512]{2,1,0:T(8,128)S(1)} %fusion.38), channel_id=1, source_target_pairs={{0,8},{8,0},{1,9},{9,1},{2,10},{10,2},{3,11},{11,3},{4,12},{12,4},... | collective-permute-start | bytes 1572872 | tf_op jit(solution)/shard_map/ppermute | solution.py:75
  18.2 7.9 %copy-start.1 = (bf16[2,1536,1024]{2,1,0:T(8,128)(2,1)}, bf16[2,1536,1024]{2,1,0:T(8,128)(2,1)S(1)}, u32[]{:S(2)}) copy-start(bf16[2,1536,1024]{2,1,0:T(8,128)(2,1)S(1)} %fusion.11) | copy-start | bytes 18874372
  20.0 5.7 %collective-permute-start.1 = (f32[8,32,1536]{2,1,0:T(8,128)S(1)}, f32[8,32,1536]{2,1,0:T(8,128)S(1)}, u32[]{:S(2)}, u32[]{:S(2)}) collective-permute-start(f32[8,32,1536]{2,1,0:T(8,128)S(1)} %fusion.28), channel_id=1, source_target_pairs={{0,8},{8,0},{1,9},{9,1},{2,10},{10,2},{3,11},{11,3},{4,12},{12,4},... | collective-permute-start | bytes 4718600 | tf_op jit(solution)/shard_map/ppermute | solution.py:76
  32.9 26.8 %collective-permute-start.2 = (f32[8,96,1536]{2,1,0:T(8,128)}, f32[8,96,1536]{2,1,0:T(8,128)}, u32[]{:S(2)}, u32[]{:S(2)}) collective-permute-start(f32[8,96,1536]{2,1,0:T(8,128)} %fusion.17), channel_id=1, source_target_pairs={{0,8},{8,0},{1,9},{9,1},{2,10},{10,2},{3,11},{11,3},{4,12},{12,4},... | collective-permute-start | bytes 14155784 | tf_op jit(solution)/shard_map/ppermute | solution.py:83
  34.3 10.5 %collective-permute-start.3 = (bf16[32,2048]{1,0:T(8,128)(2,1)}, bf16[32,2048]{1,0:T(8,128)(2,1)S(1)}, u32[]{:S(2)}, u32[]{:S(2)}) collective-permute-start(bf16[32,2048]{1,0:T(8,128)(2,1)} %get-tuple-element.26), channel_id=1, source_target_pairs={{0,16},{16,32},{32,48},{48,0},{64,80},{80,96},{96,112},{112,64},{1... | collective-permute-start | bytes 393224 | tf_op jit(solution)/shard_map/ppermute | solution.py:44
  34.8 10.4 %collective-permute-start.9 = (bf16[32,2048]{1,0:T(8,128)(2,1)}, bf16[32,2048]{1,0:T(8,128)(2,1)S(1)}, u32[]{:S(2)}, u32[]{:S(2)}) collective-permute-start(bf16[32,2048]{1,0:T(8,128)(2,1)} %get-tuple-element.27), channel_id=1, source_target_pairs={{0,112},{16,64},{32,80},{48,96},{64,48},{80,0},{96,16},{112,32},{1... | collective-permute-start | bytes 393224 | tf_op jit(solution)/shard_map/ppermute | solution.py:44
  39.0 10.5 %collective-permute-start.8 = (bf16[32,2048]{1,0:T(8,128)(2,1)}, bf16[32,2048]{1,0:T(8,128)(2,1)}, u32[]{:S(2)}, u32[]{:S(2)}) collective-permute-start(bf16[32,2048]{1,0:T(8,128)(2,1)} %get-tuple-element.28), channel_id=1, source_target_pairs={{0,96},{16,112},{32,64},{48,80},{64,32},{80,48},{96,0},{112,16},{1... | collective-permute-start | bytes 393224 | tf_op jit(solution)/shard_map/ppermute | solution.py:44
  40.1 18.4 %collective-permute-start.7 = (bf16[32,2048]{1,0:T(8,128)(2,1)}, bf16[32,2048]{1,0:T(8,128)(2,1)S(1)}, u32[]{:S(2)}, u32[]{:S(2)}) collective-permute-start(bf16[32,2048]{1,0:T(8,128)(2,1)} %get-tuple-element.29), channel_id=1, source_target_pairs={{0,80},{16,96},{32,112},{48,64},{64,16},{80,32},{96,48},{112,0},{1... | collective-permute-start | bytes 393224 | tf_op jit(solution)/shard_map/ppermute | solution.py:44
  44.9 13.7 %collective-permute-start.6 = (bf16[32,2048]{1,0:T(8,128)(2,1)}, bf16[32,2048]{1,0:T(8,128)(2,1)S(1)}, u32[]{:S(2)}, u32[]{:S(2)}) collective-permute-start(bf16[32,2048]{1,0:T(8,128)(2,1)} %get-tuple-element.30), channel_id=1, source_target_pairs={{0,64},{16,80},{32,96},{48,112},{64,0},{80,16},{96,32},{112,48},{1... | collective-permute-start | bytes 393224 | tf_op jit(solution)/shard_map/ppermute | solution.py:44
  45.2 13.4 %collective-permute-start.5 = (bf16[32,2048]{1,0:T(8,128)(2,1)}, bf16[32,2048]{1,0:T(8,128)(2,1)S(1)}, u32[]{:S(2)}, u32[]{:S(2)}) collective-permute-start(bf16[32,2048]{1,0:T(8,128)(2,1)} %get-tuple-element.31), channel_id=1, source_target_pairs={{0,48},{16,0},{32,16},{48,32},{64,112},{80,64},{96,80},{112,96},{1... | collective-permute-start | bytes 393224 | tf_op jit(solution)/shard_map/ppermute | solution.py:44
  49.5 9.1 %collective-permute-start.4 = (bf16[32,2048]{1,0:T(8,128)(2,1)S(1)}, bf16[32,2048]{1,0:T(8,128)(2,1)S(1)}, u32[]{:S(2)}, u32[]{:S(2)}) collective-permute-start(bf16[32,2048]{1,0:T(8,128)(2,1)S(1)} %get-tuple-element.32), channel_id=1, source_target_pairs={{0,32},{16,48},{32,0},{48,16},{64,96},{80,112},{96,64},{112,80},{1... | collective-permute-start | bytes 393224 | tf_op jit(solution)/shard_map/ppermute | solution.py:44
  63.1 26.2 %collective-permute-start.13 = (bf16[96,1536]{1,0:T(8,128)(2,1)S(1)}, bf16[96,1536]{1,0:T(8,128)(2,1)S(1)}, u32[]{:S(2)}, u32[]{:S(2)}) collective-permute-start(bf16[96,1536]{1,0:T(8,128)(2,1)S(1)} %get-tuple-element.17), channel_id=1, source_target_pairs={{0,16},{16,32},{32,48},{48,0},{64,80},{80,96},{96,112},{112,64},{1... | collective-permute-start | bytes 884744 | tf_op jit(solution)/shard_map/ppermute | solution.py:44
  65.8 23.5 %collective-permute-start.19 = (bf16[96,1536]{1,0:T(8,128)(2,1)S(1)}, bf16[96,1536]{1,0:T(8,128)(2,1)S(1)}, u32[]{:S(2)}, u32[]{:S(2)}) collective-permute-start(bf16[96,1536]{1,0:T(8,128)(2,1)S(1)} %get-tuple-element.18), channel_id=1, source_target_pairs={{0,112},{16,64},{32,80},{48,96},{64,48},{80,0},{96,16},{112,32},{1... | collective-permute-start | bytes 884744 | tf_op jit(solution)/shard_map/ppermute | solution.py:44
  67.8 4.3 %collective-permute-start.10 = (f32[32,512]{1,0:T(8,128)S(1)}, f32[32,512]{1,0:T(8,128)S(1)}, u32[]{:S(2)}, u32[]{:S(2)}) collective-permute-start(f32[32,512]{1,0:T(8,128)S(1)} %slice.8), channel_id=1, source_target_pairs={{0,2},{2,0},{4,6},{6,4},{1,3},{3,1},{5,7},{7,5},{8,10},{10,8},{12,... | collective-permute-start | bytes 196616 | tf_op jit(solution)/shard_map/ppermute | solution.py:108
  72.1 5.8 %collective-permute-start.11 = (f32[32,512]{1,0:T(8,128)S(1)}, f32[32,512]{1,0:T(8,128)S(1)}, u32[]{:S(2)}, u32[]{:S(2)}) collective-permute-start(f32[32,512]{1,0:T(8,128)S(1)} %add.213), channel_id=1, source_target_pairs={{0,4},{2,6},{4,0},{6,2},{1,5},{3,7},{5,1},{7,3},{8,12},{10,14},{12... | collective-permute-start | bytes 196616 | tf_op jit(solution)/shard_map/ppermute | solution.py:108
  78.0 10.2 %collective-permute-start.12 = (f32[32,512]{1,0:T(8,128)S(1)}, f32[32,512]{1,0:T(8,128)S(1)}, u32[]{:S(2)}, u32[]{:S(2)}) collective-permute-start(f32[32,512]{1,0:T(8,128)S(1)} %add.214), channel_id=1, source_target_pairs={{0,1},{1,0},{2,3},{3,2},{4,5},{5,4},{6,7},{7,6},{8,9},{9,8},{10,11... | collective-permute-start | bytes 196616 | tf_op jit(solution)/shard_map/ppermute | solution.py:108
  78.6 16.7 %collective-permute-start.18 = (bf16[96,1536]{1,0:T(8,128)(2,1)S(1)}, bf16[96,1536]{1,0:T(8,128)(2,1)S(1)}, u32[]{:S(2)}, u32[]{:S(2)}) collective-permute-start(bf16[96,1536]{1,0:T(8,128)(2,1)S(1)} %get-tuple-element.19), channel_id=1, source_target_pairs={{0,96},{16,112},{32,64},{48,80},{64,32},{80,48},{96,0},{112,16},{1... | collective-permute-start | bytes 884744 | tf_op jit(solution)/shard_map/ppermute | solution.py:44
  81.7 13.7 %collective-permute-start.17 = (bf16[96,1536]{1,0:T(8,128)(2,1)S(1)}, bf16[96,1536]{1,0:T(8,128)(2,1)S(1)}, u32[]{:S(2)}, u32[]{:S(2)}) collective-permute-start(bf16[96,1536]{1,0:T(8,128)(2,1)S(1)} %get-tuple-element.20), channel_id=1, source_target_pairs={{0,80},{16,96},{32,112},{48,64},{64,16},{80,32},{96,48},{112,0},{1... | collective-permute-start | bytes 884744 | tf_op jit(solution)/shard_map/ppermute | solution.py:44
  88.2 10.8 %collective-permute-start.16 = (bf16[96,1536]{1,0:T(8,128)(2,1)S(1)}, bf16[96,1536]{1,0:T(8,128)(2,1)S(1)}, u32[]{:S(2)}, u32[]{:S(2)}) collective-permute-start(bf16[96,1536]{1,0:T(8,128)(2,1)S(1)} %get-tuple-element.21), channel_id=1, source_target_pairs={{0,64},{16,80},{32,96},{48,112},{64,0},{80,16},{96,32},{112,48},{1... | collective-permute-start | bytes 884744 | tf_op jit(solution)/shard_map/ppermute | solution.py:44
  89.3 9.8 %collective-permute-start.15 = (bf16[96,1536]{1,0:T(8,128)(2,1)S(1)}, bf16[96,1536]{1,0:T(8,128)(2,1)S(1)}, u32[]{:S(2)}, u32[]{:S(2)}) collective-permute-start(bf16[96,1536]{1,0:T(8,128)(2,1)S(1)} %get-tuple-element.22), channel_id=1, source_target_pairs={{0,48},{16,0},{32,16},{48,32},{64,112},{80,64},{96,80},{112,96},{1... | collective-permute-start | bytes 884744 | tf_op jit(solution)/shard_map/ppermute | solution.py:44
  89.3 12.6 %collective-permute-start.14 = (bf16[96,1536]{1,0:T(8,128)(2,1)S(1)}, bf16[96,1536]{1,0:T(8,128)(2,1)S(1)}, u32[]{:S(2)}, u32[]{:S(2)}) collective-permute-start(bf16[96,1536]{1,0:T(8,128)(2,1)S(1)} %get-tuple-element.23), channel_id=1, source_target_pairs={{0,32},{16,48},{32,0},{48,16},{64,96},{80,112},{96,64},{112,80},{1... | collective-permute-start | bytes 884744 | tf_op jit(solution)/shard_map/ppermute | solution.py:44
where the time goes:
time: 103 us
  starting transfers between devices  32.4 us (31%)
  matrix products  31.9 us (31%)
  waiting for transfers between devices  22 us (21%)
  local copies, waits for them, and re-layouts  8.55 us (8%)
  other arithmetic  7.27 us (7%)
    ppermute x14, starting transfers between devices, chip_exchange(): total = total + lax.ppermute(piece, CHIP_AXES, pairs).astype(jnp.float32)  29.2 us
    dot_general x6, matrix products, gram(): lax.dot_general(first, second, (((0, first.ndim - 1), (0, second.ndim - 1...  20.1 us
    dot_general x2, matrix products, left_products(): lax.dot_general(border, factor, (((1,), (1,)), ((0,), (0,))), preferred_e...  11.8 us
    ppermute x3, waiting for transfers between devices, region_sum(): top = top + lax.ppermute(top, axis, pairs)  11.2 us
    ppermute x14, waiting for transfers between devices, chip_exchange(): total = total + lax.ppermute(piece, CHIP_AXES, pairs).astype(jnp.float32)  10.8 us
    unnamed x12, local copies, waits for them, and re-layouts  4.51 us
    convert_element_type x1, other arithmetic, shards_body(): send_ll = (own_ll + sib_ll).astype(jnp.bfloat16)  3.21 us
    dynamic_slice x2, local copies, waits for them, and re-layouts, pick(): return lax.dynamic_index_in_dim(by_owner, which, 2, keepdims=False)  3 us
  transfers between devices with their start and end apart: 20, of which 6 were waited for; matrix products, arithmetic and copies ran while one was open for 25% of the time, Pallas kernels for 0%

commit v1 on v0

--- a/solution.py
+++ b/solution.py
@@ -79,8 +79,7 @@
     send_top = jnp.concatenate([own_gg + sib_gg, own_gl + sib_gl], axis=2).astype(jnp.bfloat16)
     send_top, late_l = lax.optimization_barrier((send_top, left_l))
     summed_top = chip_exchange(send_top)
-    sib_ll_part = gram(pick(by_owner_l, 1 - core), late_l)
-    sib_ll = lax.ppermute(sib_ll_part, "core", swap)
+    sib_ll = lax.ppermute(gram(pick(by_owner_l, 1 - core), late_l), "core", swap)
     own_ll = lax.optimization_barrier(gram(pick(by_owner_l, core), late_l))
     send_ll = (own_ll + sib_ll).astype(jnp.bfloat16)
     top_rows = summed_top[:, :global_cols]
@@ -105,6 +104,8 @@
         step = 1
         while step < size:
             pairs = [(i, i ^ step) for i in range(size)]
+            if size == 4 and step == 2:
+                pairs = [(i, size - 1 - i) for i in range(size)]
             top = top + lax.ppermute(top, axis, pairs)
             step *= 2
     return top

time: 103 us -> 103 us (level)
  the two profiles are of different devices: /device:TPU:70 before, /device:TPU:0 now
where the time goes in v1:
time: 103 us
  starting transfers between devices  36.4 us (35%)
  matrix products  31.9 us (31%)
  waiting for transfers between devices  18 us (17%)
  local copies, waits for them, and re-layouts  8.54 us (8%)
  other arithmetic  7.27 us (7%)
    ppermute x14, starting transfers between devices, chip_exchange(): total = total + lax.ppermute(piece, CHIP_AXES, pairs).astype(jnp.float32)  28.9 us
    dot_general x6, matrix products, gram(): lax.dot_general(first, second, (((0, first.ndim - 1), (0, second.ndim - 1...  20.1 us
    dot_general x2, matrix products, left_products(): lax.dot_general(border, factor, (((1,), (1,)), ((0,), (0,))), preferred_e...  11.8 us
    ppermute x14, waiting for transfers between devices, chip_exchange(): total = total + lax.ppermute(piece, CHIP_AXES, pairs).astype(jnp.float32)  9.01 us
    ppermute x3, waiting for transfers between devices, region_sum(): top = top + lax.ppermute(top, axis, pairs)  9.01 us
    ppermute x3, starting transfers between devices, region_sum(): top = top + lax.ppermute(top, axis, pairs)  6.61 us
    unnamed x12, local copies, waits for them, and re-layouts  4.5 us
    convert_element_type x1, other arithmetic, shards_body(): send_ll = (own_ll + sib_ll).astype(jnp.bfloat16)  3.21 us
  transfers between devices with their start and end apart: 20, of which 8 were waited for; matrix products, arithmetic and copies ran while one was open for 25% of the time, Pallas kernels for 0%

profile of v1, /device:TPU:0, one launch (start us, length us, event | category | flops | bytes accessed | tf_op | source)
XLA Modules:
  0.0 103.0 jit_solution(7704187534665885425)
XLA Ops:
  0.6 0.0 copy-start
  0.7 1.6 %copy-done = bf16[2,1024,512]{2,1,0:T(8,128)(2,1)S(1)} copy-done((bf16[2,1024,512]{2,1,0:T(8,128)(2,1)S(1)}, bf16[2,1024,512]{2,1,0:T(8,128)(2,1)}, u32[]{:S(2)}) %copy-start) | copy-done | bytes 2097176
  2.2 4.5 %convolution_convert_fusion = bf16[2,512,1024]{2,1,0:T(8,128)(2,1)S(1)} fusion(bf16[2,1024,512]{2,1,0:T(8,128)(2,1)S(1)} %copy-done, bf16[2,1024,1024]{2,1,0:T(8,128)(2,1)} %param.4), kind=kOutput, calls=%fused_computation.26 | convolution fusion | flops 2148532224 | bytes 8388608 | tf_op jit(solution)/shard_map/dot_general | solution.py:17
  6.8 0.0 slice-start
  6.8 0.3 constant_dynamic-slice_fusion.1
  7.1 0.0 copy-start.2
  7.1 0.0 slice-start.1
  7.1 0.0 copy-start.3
  7.1 0.7 fusion.38
  7.9 0.1 collective-permute-start
  8.0 0.1 iota_compare_fusion
  8.1 0.9 slice-done
  9.0 0.8 slice-done.1
  9.7 1.2 %copy-done.3 = bf16[2,1024,1024]{2,1,0:T(8,128)(2,1)S(1)} copy-done((bf16[2,1024,1024]{2,1,0:T(8,128)(2,1)S(1)}, bf16[2,1024,1024]{2,1,0:T(8,128)(2,1)}, u32[]{:S(2)}) %copy-start.3) | copy-done | bytes 4194328
  10.9 7.2 %fusion.11 = bf16[2,1536,1024]{2,1,0:T(8,128)(2,1)S(1)} fusion(bf16[2,1024,1024]{2,1,0:T(8,128)(2,1)S(1)} %copy-done.3, bf16[2,1024,1536]{2,1,0:T(8,128)(2,1)S(1)} %bitcast.107, pred[2,1536]{1,0:T(4,128)(4,1)S(1)} %iota_compare_fusion), kind=kOutput, calls=%fused_computation.11 | convolution fusion | flops 6448742400 | bytes 16780288 | tf_op jit(solution)/shard_map/dot_general | solution.py:17
  18.2 1.8 %fusion.28 = f32[8,32,1536]{2,1,0:T(8,128)S(1)} fusion(bf16[2,1536,1024]{2,1,0:T(8,128)(2,1)S(1)} %fusion.11, bf16[2,8,1,32,1024]{4,3,2,1,0:T(8,128)(2,1)S(1)} %get-tuple-element.24), kind=kOutput, calls=%fused_computation.21 | convolution fusion | flops 1610612736 | bytes 8912896 | tf_op jit(solution)/shard_map/dot_general | solution.py:23
  20.0 0.3 collective-permute-start.1
  20.3 1.8 %fusion.25 = f32[8,32,1536]{2,1,0:T(8,128)S(1)} fusion(bf16[2,1536,1024]{2,1,0:T(8,128)(2,1)S(1)} %fusion.11, bf16[2,8,1,32,1024]{4,3,2,1,0:T(8,128)(2,1)S(1)} %get-tuple-element.25), kind=kOutput, calls=%fused_computation.20 | convolution fusion | flops 1610612736 | bytes 8912896 | tf_op jit(solution)/shard_map/dot_general | solution.py:23
  22.1 0.7 fusion.35
  22.9 2.7 %constant_dynamic-slice_fusion = (bf16[2,8,1,96,1024]{4,3,2,1,0:T(8,128)(2,1)S(1)}, bf16[2,8,1,96,1024]{4,3,2,1,0:T(8,128)(2,1)}) fusion(bf16[2,8,2,96,1024]{4,3,2,1,0:T(8,128)(2,1)S(1)} %bitcast.104, s32[]{:T(128)S(6)} %select_n.89, s32[]{:T(128)S(6)} %select_n.88), kind=kLoop, calls=%fused_computation.74 | loop fusion | bytes 12582920 | tf_op jit(solution)/shard_map/jit(dynamic_index_in_dim)/dynamic_slice | solution.py:71
  25.6 0.0 collective-permute-done
  25.6 0.1 add_convert_fusion.2
  25.7 0.0 collective-permute-done.1
  25.7 0.2 add_convert_fusion.1
  25.9 0.1 pad_maximum_fusion
  26.1 6.8 %fusion.17 = f32[8,96,1536]{2,1,0:T(8,128)} fusion(bf16[2,1536,1024]{2,1,0:T(8,128)(2,1)S(1)} %fusion.11, bf16[2,8,1,96,1024]{4,3,2,1,0:T(8,128)(2,1)S(1)} %get-tuple-element.15), kind=kOutput, calls=%fused_computation.14 | convolution fusion | flops 4831838208 | bytes 14155776 | tf_op jit(solution)/shard_map/dot_general | solution.py:23
  32.9 0.5 collective-permute-start.2
  33.4 0.9 dynamic-slice_bitcast_fusion.13
  34.3 1.6 %collective-permute-start.3 = (bf16[32,2048]{1,0:T(8,128)(2,1)}, bf16[32,2048]{1,0:T(8,128)(2,1)S(1)}, u32[]{:S(2)}, u32[]{:S(2)}) collective-permute-start(bf16[32,2048]{1,0:T(8,128)(2,1)} %get-tuple-element.26), channel_id=1, source_target_pairs={{0,16},{16,32},{32,48},{48,0},{64,80},{80,96},{96,112},{112,64},{1... | collective-permute-start | bytes 393224 | tf_op jit(solution)/shard_map/ppermute | solution.py:44
  35.9 4.4 %collective-permute-start.9 = (bf16[32,2048]{1,0:T(8,128)(2,1)}, bf16[32,2048]{1,0:T(8,128)(2,1)S(1)}, u32[]{:S(2)}, u32[]{:S(2)}) collective-permute-start(bf16[32,2048]{1,0:T(8,128)(2,1)} %get-tuple-element.27), channel_id=1, source_target_pairs={{0,112},{16,64},{32,80},{48,96},{64,48},{80,0},{96,16},{112,32},{1... | collective-permute-start | bytes 393224 | tf_op jit(solution)/shard_map/ppermute | solution.py:44
  40.3 1.6 %collective-permute-start.8 = (bf16[32,2048]{1,0:T(8,128)(2,1)}, bf16[32,2048]{1,0:T(8,128)(2,1)}, u32[]{:S(2)}, u32[]{:S(2)}) collective-permute-start(bf16[32,2048]{1,0:T(8,128)(2,1)} %get-tuple-element.28), channel_id=1, source_target_pairs={{0,96},{16,112},{32,64},{48,80},{64,32},{80,48},{96,0},{112,16},{1... | collective-permute-start | bytes 393224 | tf_op jit(solution)/shard_map/ppermute | solution.py:44
  41.8 3.2 %collective-permute-start.7 = (bf16[32,2048]{1,0:T(8,128)(2,1)}, bf16[32,2048]{1,0:T(8,128)(2,1)S(1)}, u32[]{:S(2)}, u32[]{:S(2)}) collective-permute-start(bf16[32,2048]{1,0:T(8,128)(2,1)} %get-tuple-element.29), channel_id=1, source_target_pairs={{0,80},{16,96},{32,112},{48,64},{64,16},{80,32},{96,48},{112,0},{1... | collective-permute-start | bytes 393224 | tf_op jit(solution)/shard_map/ppermute | solution.py:44
  45.1 0.0 collective-permute-done.3
  45.1 0.3 collective-permute-start.6
  45.4 0.7 collective-permute-done.9
  46.1 2.0 %collective-permute-start.5 = (bf16[32,2048]{1,0:T(8,128)(2,1)}, bf16[32,2048]{1,0:T(8,128)(2,1)S(1)}, u32[]{:S(2)}, u32[]{:S(2)}) collective-permute-start(bf16[32,2048]{1,0:T(8,128)(2,1)} %get-tuple-element.31), channel_id=1, source_target_pairs={{0,48},{16,0},{32,16},{48,32},{64,112},{80,64},{96,80},{112,96},{1... | collective-permute-start | bytes 393224 | tf_op jit(solution)/shard_map/ppermute | solution.py:44
  48.1 2.8 %collective-permute-done.8 = bf16[32,2048]{1,0:T(8,128)(2,1)} collective-permute-done((bf16[32,2048]{1,0:T(8,128)(2,1)}, bf16[32,2048]{1,0:T(8,128)(2,1)}, u32[]{:S(2)}, u32[]{:S(2)}) %collective-permute-start.8) | collective-permute-done | bytes 131104 | tf_op jit(solution)/shard_map/ppermute | solution.py:44
  50.9 1.9 %collective-permute-start.4 = (bf16[32,2048]{1,0:T(8,128)(2,1)S(1)}, bf16[32,2048]{1,0:T(8,128)(2,1)S(1)}, u32[]{:S(2)}, u32[]{:S(2)}) collective-permute-start(bf16[32,2048]{1,0:T(8,128)(2,1)S(1)} %get-tuple-element.32), channel_id=1, source_target_pairs={{0,32},{16,48},{32,0},{48,16},{64,96},{80,112},{96,64},{112,80},{1... | collective-permute-start | bytes 393224 | tf_op jit(solution)/shard_map/ppermute | solution.py:44
  52.7 8.2 %fusion.14 = f32[8,96,1536]{2,1,0:T(8,128)S(1)} fusion(bf16[2,1536,1024]{2,1,0:T(8,128)(2,1)} %copy-done.1, bf16[2,8,1,96,1024]{4,3,2,1,0:T(8,128)(2,1)} %get-tuple-element.16), kind=kOutput, calls=%fused_computation.13 | convolution fusion | flops 4831838208 | bytes 14155776 | tf_op jit(solution)/shard_map/dot_general | solution.py:23
  60.9 0.0 collective-permute-done.7
  60.9 0.0 collective-permute-done.6
  60.9 0.0 collective-permute-done.4
  60.9 1.0 %fusion.62 = f32[32,2048]{1,0:T(8,128)S(1)} fusion(bf16[32,2048]{1,0:T(8,128)(2,1)S(1)} %collective-permute-done.9, bf16[32,2048]{1,0:T(8,128)(2,1)} %collective-permute-done.8, bf16[32,2048]{1,0:T(8,128)(2,1)S(1)} %collective-permute-done.7, bf16[32,2048]{1,0:T(8,128)(2,1)S(1)} %collective-permute-done.6, bf16[32,2048]{1,0:T(8,128)(2,1)S(1)} %collective-permute-done.5, ...), kind=kLoop, calls=%fused_computation.62 | loop fusion | flops 983040 | bytes 1310724 | tf_op jit(solution)/shard_map/add | solution.py:44
  62.0 3.2 %add_convert_fusion = bf16[8,96,1536]{2,1,0:T(8,128)(2,1)S(1)} fusion(f32[8,96,1536]{2,1,0:T(8,128)S(1)} %fusion.14, f32[8,96,1536]{2,1,0:T(8,128)} %collective-permute-done.2), kind=kLoop, calls=%fused_computation.12 | loop fusion | flops 2359296 | bytes 11796480 | tf_op jit(solution)/shard_map/convert_element_type | solution.py:84
  65.2 0.2 dynamic-slice_bitcast_fusion.6
  65.4 0.5 collective-permute-start.13
  65.9 3.7 %collective-permute-start.19 = (bf16[96,1536]{1,0:T(8,128)(2,1)S(1)}, bf16[96,1536]{1,0:T(8,128)(2,1)S(1)}, u32[]{:S(2)}, u32[]{:S(2)}) collective-permute-start(bf16[96,1536]{1,0:T(8,128)(2,1)S(1)} %get-tuple-element.18), channel_id=1, source_target_pairs={{0,112},{16,64},{32,80},{48,96},{64,48},{80,0},{96,16},{112,32},{1... | collective-permute-start | bytes 884744 | tf_op jit(solution)/shard_map/ppermute | solution.py:44
  69.6 1.9 %collective-permute-start.10 = (f32[32,512]{1,0:T(8,128)S(1)}, f32[32,512]{1,0:T(8,128)S(1)}, u32[]{:S(2)}, u32[]{:S(2)}) collective-permute-start(f32[32,512]{1,0:T(8,128)S(1)} %slice.8), channel_id=1, source_target_pairs={{0,2},{2,0},{4,6},{6,4},{1,3},{3,1},{5,7},{7,5},{8,10},{10,8},{12,... | collective-permute-start | bytes 196616 | tf_op jit(solution)/shard_map/ppermute | solution.py:109
  71.5 2.4 %collective-permute-done.10 = f32[32,512]{1,0:T(8,128)S(1)} collective-permute-done((f32[32,512]{1,0:T(8,128)S(1)}, f32[32,512]{1,0:T(8,128)S(1)}, u32[]{:S(2)}, u32[]{:S(2)}) %collective-permute-start.10) | collective-permute-done | bytes 65568 | tf_op jit(solution)/shard_map/ppermute | solution.py:109
  73.9 4.1 %collective-permute-start.11 = (f32[32,512]{1,0:T(8,128)S(1)}, f32[32,512]{1,0:T(8,128)S(1)}, u32[]{:S(2)}, u32[]{:S(2)}) collective-permute-start(f32[32,512]{1,0:T(8,128)S(1)} %add.213), channel_id=1, source_target_pairs={{0,6},{2,4},{4,2},{6,0},{1,7},{3,5},{5,3},{7,1},{8,14},{10,12},{12... | collective-permute-start | bytes 196616 | tf_op jit(solution)/shard_map/ppermute | solution.py:109
  78.0 2.2 %collective-permute-done.11 = f32[32,512]{1,0:T(8,128)S(1)} collective-permute-done((f32[32,512]{1,0:T(8,128)S(1)}, f32[32,512]{1,0:T(8,128)S(1)}, u32[]{:S(2)}, u32[]{:S(2)}) %collective-permute-start.11) | collective-permute-done | bytes 65568 | tf_op jit(solution)/shard_map/ppermute | solution.py:109
  80.3 0.6 collective-permute-start.12
  80.9 2.8 %collective-permute-start.18 = (bf16[96,1536]{1,0:T(8,128)(2,1)S(1)}, bf16[96,1536]{1,0:T(8,128)(2,1)S(1)}, u32[]{:S(2)}, u32[]{:S(2)}) collective-permute-start(bf16[96,1536]{1,0:T(8,128)(2,1)S(1)} %get-tuple-element.19), channel_id=1, source_target_pairs={{0,96},{16,112},{32,64},{48,80},{64,32},{80,48},{96,0},{112,16},{1... | collective-permute-start | bytes 884744 | tf_op jit(solution)/shard_map/ppermute | solution.py:44
  83.6 1.6 %collective-permute-start.17 = (bf16[96,1536]{1,0:T(8,128)(2,1)S(1)}, bf16[96,1536]{1,0:T(8,128)(2,1)S(1)}, u32[]{:S(2)}, u32[]{:S(2)}) collective-permute-start(bf16[96,1536]{1,0:T(8,128)(2,1)S(1)} %get-tuple-element.20), channel_id=1, source_target_pairs={{0,80},{16,96},{32,112},{48,64},{64,16},{80,32},{96,48},{112,0},{1... | collective-permute-start | bytes 884744 | tf_op jit(solution)/shard_map/ppermute | solution.py:44
  85.3 4.4 %collective-permute-done.12 = f32[32,512]{1,0:T(8,128)S(1)} collective-permute-done((f32[32,512]{1,0:T(8,128)S(1)}, f32[32,512]{1,0:T(8,128)S(1)}, u32[]{:S(2)}, u32[]{:S(2)}) %collective-permute-start.12) | collective-permute-done | bytes 65568 | tf_op jit(solution)/shard_map/ppermute | solution.py:109
  89.7 2.0 %collective-permute-start.16 = (bf16[96,1536]{1,0:T(8,128)(2,1)S(1)}, bf16[96,1536]{1,0:T(8,128)(2,1)S(1)}, u32[]{:S(2)}, u32[]{:S(2)}) collective-permute-start(bf16[96,1536]{1,0:T(8,128)(2,1)S(1)} %get-tuple-element.21), channel_id=1, source_target_pairs={{0,64},{16,80},{32,96},{48,112},{64,0},{80,16},{96,32},{112,48},{1... | collective-permute-start | bytes 884744 | tf_op jit(solution)/shard_map/ppermute | solution.py:44
  91.6 2.0 %collective-permute-start.15 = (bf16[96,1536]{1,0:T(8,128)(2,1)S(1)}, bf16[96,1536]{1,0:T(8,128)(2,1)S(1)}, u32[]{:S(2)}, u32[]{:S(2)}) collective-permute-start(bf16[96,1536]{1,0:T(8,128)(2,1)S(1)} %get-tuple-element.22), channel_id=1, source_target_pairs={{0,48},{16,0},{32,16},{48,32},{64,112},{80,64},{96,80},{112,96},{1... | collective-permute-start | bytes 884744 | tf_op jit(solution)/shard_map/ppermute | solution.py:44
  93.6 1.4 %collective-permute-start.14 = (bf16[96,1536]{1,0:T(8,128)(2,1)S(1)}, bf16[96,1536]{1,0:T(8,128)(2,1)S(1)}, u32[]{:S(2)}, u32[]{:S(2)}) collective-permute-start(bf16[96,1536]{1,0:T(8,128)(2,1)S(1)} %get-tuple-element.23), channel_id=1, source_target_pairs={{0,32},{16,48},{32,0},{48,16},{64,96},{80,112},{96,64},{112,80},{1... | collective-permute-start | bytes 884744 | tf_op jit(solution)/shard_map/ppermute | solution.py:44
  95.0 0.7 fusion.63
  95.7 0.6 add_multiply_fusion
  96.3 2.3 %collective-permute-done.17 = bf16[96,1536]{1,0:T(8,128)(2,1)S(1)} collective-permute-done((bf16[96,1536]{1,0:T(8,128)(2,1)S(1)}, bf16[96,1536]{1,0:T(8,128)(2,1)S(1)}, u32[]{:S(2)}, u32[]{:S(2)}) %collective-permute-start.17) | collective-permute-done | bytes 294944 | tf_op jit(solution)/shard_map/ppermute | solution.py:44
  98.6 2.9 %collective-permute-done.16 = bf16[96,1536]{1,0:T(8,128)(2,1)S(1)} collective-permute-done((bf16[96,1536]{1,0:T(8,128)(2,1)S(1)}, bf16[96,1536]{1,0:T(8,128)(2,1)S(1)}, u32[]{:S(2)}, u32[]{:S(2)}) %collective-permute-start.16) | collective-permute-done | bytes 294944 | tf_op jit(solution)/shard_map/ppermute | solution.py:44
  101.5 0.4 collective-permute-done.14
  101.9 1.1 %fusion.56 = f32[1,96,1536]{2,1,0:T(8,128)} fusion(bf16[96,1536]{1,0:T(8,128)(2,1)S(1)} %collective-permute-done.19, bf16[96,1536]{1,0:T(8,128)(2,1)S(1)} %collective-permute-done.18, bf16[96,1536]{1,0:T(8,128)(2,1)S(1)} %collective-permute-done.17, bf16[96,1536]{1,0:T(8,128)(2,1)S(1)} %collective-permute-done.16, ...), kind=kLoop, calls=%fused_computation.47 | loop fusion | flops 2359296 | bytes 2949124 | tf_op jit(solution)/shard_map/broadcast_in_dim | solution.py:96
  (13 shorter events, 0.0 us)
Async XLA Ops:
  0.6 1.6 %copy-start = (bf16[2,1024,512]{2,1,0:T(8,128)(2,1)S(1)}, bf16[2,1024,512]{2,1,0:T(8,128)(2,1)}, u32[]{:S(2)}) copy-start(bf16[2,1024,512]{2,1,0:T(8,128)(2,1)} %param.5) | copy-start | bytes 6291460
  6.8 2.2 %slice-start = ((s8[6291456]{0:T(1024)(128)(4,1)}), s8[4194304]{0:T(1024)(128)(4,1)S(1)}, s32[]{:S(2)}) async-start(s8[6291456]{0:T(1024)(128)(4,1)} %bitcast.106), calls=%async_computation | async-start | bytes 8388608
  7.1 0.9 copy-start.2
  7.1 2.7 %slice-start.1 = ((s8[6291456]{0:T(1024)(128)(4,1)}), s8[2097152]{0:T(1024)(128)(4,1)S(1)}, s32[]{:S(2)}) async-start(s8[6291456]{0:T(1024)(128)(4,1)} %bitcast.106), calls=%async_computation.1 | async-start | bytes 4194304
  7.1 3.8 %copy-start.3 = (bf16[2,1024,1024]{2,1,0:T(8,128)(2,1)S(1)}, bf16[2,1024,1024]{2,1,0:T(8,128)(2,1)}, u32[]{:S(2)}) copy-start(bf16[2,1024,1024]{2,1,0:T(8,128)(2,1)} %param.4) | copy-start | bytes 12582916
  7.9 17.7 %collective-permute-start = (f32[8,32,512]{2,1,0:T(8,128)S(1)}, f32[8,32,512]{2,1,0:T(8,128)S(1)}, u32[]{:S(2)}, u32[]{:S(2)}) collective-permute-start(f32[8,32,512]{2,1,0:T(8,128)S(1)} %fusion.38), channel_id=1, source_target_pairs={{0,8},{8,0},{1,9},{9,1},{2,10},{10,2},{3,11},{11,3},{4,12},{12,4},... | collective-permute-start | bytes 1572872 | tf_op jit(solution)/shard_map/ppermute | solution.py:75
  18.2 7.9 %copy-start.1 = (bf16[2,1536,1024]{2,1,0:T(8,128)(2,1)}, bf16[2,1536,1024]{2,1,0:T(8,128)(2,1)S(1)}, u32[]{:S(2)}) copy-start(bf16[2,1536,1024]{2,1,0:T(8,128)(2,1)S(1)} %fusion.11) | copy-start | bytes 18874372
  20.0 5.7 %collective-permute-start.1 = (f32[8,32,1536]{2,1,0:T(8,128)S(1)}, f32[8,32,1536]{2,1,0:T(8,128)S(1)}, u32[]{:S(2)}, u32[]{:S(2)}) collective-permute-start(f32[8,32,1536]{2,1,0:T(8,128)S(1)} %fusion.28), channel_id=1, source_target_pairs={{0,8},{8,0},{1,9},{9,1},{2,10},{10,2},{3,11},{11,3},{4,12},{12,4},... | collective-permute-start | bytes 4718600 | tf_op jit(solution)/shard_map/ppermute | solution.py:76
  32.9 29.1 %collective-permute-start.2 = (f32[8,96,1536]{2,1,0:T(8,128)}, f32[8,96,1536]{2,1,0:T(8,128)}, u32[]{:S(2)}, u32[]{:S(2)}) collective-permute-start(f32[8,96,1536]{2,1,0:T(8,128)} %fusion.17), channel_id=1, source_target_pairs={{0,8},{8,0},{1,9},{9,1},{2,10},{10,2},{3,11},{11,3},{4,12},{12,4},... | collective-permute-start | bytes 14155784 | tf_op jit(solution)/shard_map/ppermute | solution.py:82
  34.3 10.8 %collective-permute-start.3 = (bf16[32,2048]{1,0:T(8,128)(2,1)}, bf16[32,2048]{1,0:T(8,128)(2,1)S(1)}, u32[]{:S(2)}, u32[]{:S(2)}) collective-permute-start(bf16[32,2048]{1,0:T(8,128)(2,1)} %get-tuple-element.26), channel_id=1, source_target_pairs={{0,16},{16,32},{32,48},{48,0},{64,80},{80,96},{96,112},{112,64},{1... | collective-permute-start | bytes 393224 | tf_op jit(solution)/shard_map/ppermute | solution.py:44
  35.9 10.2 %collective-permute-start.9 = (bf16[32,2048]{1,0:T(8,128)(2,1)}, bf16[32,2048]{1,0:T(8,128)(2,1)S(1)}, u32[]{:S(2)}, u32[]{:S(2)}) collective-permute-start(bf16[32,2048]{1,0:T(8,128)(2,1)} %get-tuple-element.27), channel_id=1, source_target_pairs={{0,112},{16,64},{32,80},{48,96},{64,48},{80,0},{96,16},{112,32},{1... | collective-permute-start | bytes 393224 | tf_op jit(solution)/shard_map/ppermute | solution.py:44
  40.3 10.6 %collective-permute-start.8 = (bf16[32,2048]{1,0:T(8,128)(2,1)}, bf16[32,2048]{1,0:T(8,128)(2,1)}, u32[]{:S(2)}, u32[]{:S(2)}) collective-permute-start(bf16[32,2048]{1,0:T(8,128)(2,1)} %get-tuple-element.28), channel_id=1, source_target_pairs={{0,96},{16,112},{32,64},{48,80},{64,32},{80,48},{96,0},{112,16},{1... | collective-permute-start | bytes 393224 | tf_op jit(solution)/shard_map/ppermute | solution.py:44
  41.8 19.0 %collective-permute-start.7 = (bf16[32,2048]{1,0:T(8,128)(2,1)}, bf16[32,2048]{1,0:T(8,128)(2,1)S(1)}, u32[]{:S(2)}, u32[]{:S(2)}) collective-permute-start(bf16[32,2048]{1,0:T(8,128)(2,1)} %get-tuple-element.29), channel_id=1, source_target_pairs={{0,80},{16,96},{32,112},{48,64},{64,16},{80,32},{96,48},{112,0},{1... | collective-permute-start | bytes 393224 | tf_op jit(solution)/shard_map/ppermute | solution.py:44
  45.1 15.8 %collective-permute-start.6 = (bf16[32,2048]{1,0:T(8,128)(2,1)}, bf16[32,2048]{1,0:T(8,128)(2,1)S(1)}, u32[]{:S(2)}, u32[]{:S(2)}) collective-permute-start(bf16[32,2048]{1,0:T(8,128)(2,1)} %get-tuple-element.30), channel_id=1, source_target_pairs={{0,64},{16,80},{32,96},{48,112},{64,0},{80,16},{96,32},{112,48},{1... | collective-permute-start | bytes 393224 | tf_op jit(solution)/shard_map/ppermute | solution.py:44
  46.1 14.8 %collective-permute-start.5 = (bf16[32,2048]{1,0:T(8,128)(2,1)}, bf16[32,2048]{1,0:T(8,128)(2,1)S(1)}, u32[]{:S(2)}, u32[]{:S(2)}) collective-permute-start(bf16[32,2048]{1,0:T(8,128)(2,1)} %get-tuple-element.31), channel_id=1, source_target_pairs={{0,48},{16,0},{32,16},{48,32},{64,112},{80,64},{96,80},{112,96},{1... | collective-permute-start | bytes 393224 | tf_op jit(solution)/shard_map/ppermute | solution.py:44
  50.9 10.1 %collective-permute-start.4 = (bf16[32,2048]{1,0:T(8,128)(2,1)S(1)}, bf16[32,2048]{1,0:T(8,128)(2,1)S(1)}, u32[]{:S(2)}, u32[]{:S(2)}) collective-permute-start(bf16[32,2048]{1,0:T(8,128)(2,1)S(1)} %get-tuple-element.32), channel_id=1, source_target_pairs={{0,32},{16,48},{32,0},{48,16},{64,96},{80,112},{96,64},{112,80},{1... | collective-permute-start | bytes 393224 | tf_op jit(solution)/shard_map/ppermute | solution.py:44
  65.4 26.3 %collective-permute-start.13 = (bf16[96,1536]{1,0:T(8,128)(2,1)S(1)}, bf16[96,1536]{1,0:T(8,128)(2,1)S(1)}, u32[]{:S(2)}, u32[]{:S(2)}) collective-permute-start(bf16[96,1536]{1,0:T(8,128)(2,1)S(1)} %get-tuple-element.17), channel_id=1, source_target_pairs={{0,16},{16,32},{32,48},{48,0},{64,80},{80,96},{96,112},{112,64},{1... | collective-permute-start | bytes 884744 | tf_op jit(solution)/shard_map/ppermute | solution.py:44
  65.9 27.8 %collective-permute-start.19 = (bf16[96,1536]{1,0:T(8,128)(2,1)S(1)}, bf16[96,1536]{1,0:T(8,128)(2,1)S(1)}, u32[]{:S(2)}, u32[]{:S(2)}) collective-permute-start(bf16[96,1536]{1,0:T(8,128)(2,1)S(1)} %get-tuple-element.18), channel_id=1, source_target_pairs={{0,112},{16,64},{32,80},{48,96},{64,48},{80,0},{96,16},{112,32},{1... | collective-permute-start | bytes 884744 | tf_op jit(solution)/shard_map/ppermute | solution.py:44
  69.6 4.3 %collective-permute-start.10 = (f32[32,512]{1,0:T(8,128)S(1)}, f32[32,512]{1,0:T(8,128)S(1)}, u32[]{:S(2)}, u32[]{:S(2)}) collective-permute-start(f32[32,512]{1,0:T(8,128)S(1)} %slice.8), channel_id=1, source_target_pairs={{0,2},{2,0},{4,6},{6,4},{1,3},{3,1},{5,7},{7,5},{8,10},{10,8},{12,... | collective-permute-start | bytes 196616 | tf_op jit(solution)/shard_map/ppermute | solution.py:109
  73.9 6.4 %collective-permute-start.11 = (f32[32,512]{1,0:T(8,128)S(1)}, f32[32,512]{1,0:T(8,128)S(1)}, u32[]{:S(2)}, u32[]{:S(2)}) collective-permute-start(f32[32,512]{1,0:T(8,128)S(1)} %add.213), channel_id=1, source_target_pairs={{0,6},{2,4},{4,2},{6,0},{1,7},{3,5},{5,3},{7,1},{8,14},{10,12},{12... | collective-permute-start | bytes 196616 | tf_op jit(solution)/shard_map/ppermute | solution.py:109
  80.3 9.4 %collective-permute-start.12 = (f32[32,512]{1,0:T(8,128)S(1)}, f32[32,512]{1,0:T(8,128)S(1)}, u32[]{:S(2)}, u32[]{:S(2)}) collective-permute-start(f32[32,512]{1,0:T(8,128)S(1)} %add.214), channel_id=1, source_target_pairs={{0,1},{1,0},{2,3},{3,2},{4,5},{5,4},{6,7},{7,6},{8,9},{9,8},{10,11... | collective-permute-start | bytes 196616 | tf_op jit(solution)/shard_map/ppermute | solution.py:109
  80.9 15.5 %collective-permute-start.18 = (bf16[96,1536]{1,0:T(8,128)(2,1)S(1)}, bf16[96,1536]{1,0:T(8,128)(2,1)S(1)}, u32[]{:S(2)}, u32[]{:S(2)}) collective-permute-start(bf16[96,1536]{1,0:T(8,128)(2,1)S(1)} %get-tuple-element.19), channel_id=1, source_target_pairs={{0,96},{16,112},{32,64},{48,80},{64,32},{80,48},{96,0},{112,16},{1... | collective-permute-start | bytes 884744 | tf_op jit(solution)/shard_map/ppermute | solution.py:44
  83.6 15.0 %collective-permute-start.17 = (bf16[96,1536]{1,0:T(8,128)(2,1)S(1)}, bf16[96,1536]{1,0:T(8,128)(2,1)S(1)}, u32[]{:S(2)}, u32[]{:S(2)}) collective-permute-start(bf16[96,1536]{1,0:T(8,128)(2,1)S(1)} %get-tuple-element.20), channel_id=1, source_target_pairs={{0,80},{16,96},{32,112},{48,64},{64,16},{80,32},{96,48},{112,0},{1... | collective-permute-start | bytes 884744 | tf_op jit(solution)/shard_map/ppermute | solution.py:44
  89.7 11.8 %collective-permute-start.16 = (bf16[96,1536]{1,0:T(8,128)(2,1)S(1)}, bf16[96,1536]{1,0:T(8,128)(2,1)S(1)}, u32[]{:S(2)}, u32[]{:S(2)}) collective-permute-start(bf16[96,1536]{1,0:T(8,128)(2,1)S(1)} %get-tuple-element.21), channel_id=1, source_target_pairs={{0,64},{16,80},{32,96},{48,112},{64,0},{80,16},{96,32},{112,48},{1... | collective-permute-start | bytes 884744 | tf_op jit(solution)/shard_map/ppermute | solution.py:44
  91.6 9.9 %collective-permute-start.15 = (bf16[96,1536]{1,0:T(8,128)(2,1)S(1)}, bf16[96,1536]{1,0:T(8,128)(2,1)S(1)}, u32[]{:S(2)}, u32[]{:S(2)}) collective-permute-start(bf16[96,1536]{1,0:T(8,128)(2,1)S(1)} %get-tuple-element.22), channel_id=1, source_target_pairs={{0,48},{16,0},{32,16},{48,32},{64,112},{80,64},{96,80},{112,96},{1... | collective-permute-start | bytes 884744 | tf_op jit(solution)/shard_map/ppermute | solution.py:44
  93.6 8.2 %collective-permute-start.14 = (bf16[96,1536]{1,0:T(8,128)(2,1)S(1)}, bf16[96,1536]{1,0:T(8,128)(2,1)S(1)}, u32[]{:S(2)}, u32[]{:S(2)}) collective-permute-start(bf16[96,1536]{1,0:T(8,128)(2,1)S(1)} %get-tuple-element.23), channel_id=1, source_target_pairs={{0,32},{16,48},{32,0},{48,16},{64,96},{80,112},{96,64},{112,80},{1... | collective-permute-start | bytes 884744 | tf_op jit(solution)/shard_map/ppermute | solution.py:44
